TPU v7x, 32 devices: a whole 2x2x4 slice. The times are simulated.
32 devices in a mesh: node: 8 (over y, x, core), hub: 4 (over z).
Axes of the slice: x: 2, y: 2, z: 4, core: 2. Of those that a mesh axis runs over, the one named last changes fastest.
Arguments:
- seed_scores: bfloat16 [32768, 128], P(('node', 'hub')), may hold values from -10 to 10
- seed_mask: int32 [32768], P(('node', 'hub')), may hold values 0 or 1
- band_offsets: int32 [256, 10], P(('node', 'hub')), may hold values from -2 to 2
- band_tiles: bfloat16 [256, 10, 128, 128], P(('node', 'hub')), may hold values from 5e-05 to 1
- hub_blocks: int32 [256, 6], P(('node', 'hub')), may hold values from 0 to 31
- hub_tiles: bfloat16 [256, 6, 128, 128], P(('node', 'hub')), may hold values from 5e-05 to 1
- hub_rows: int32 [4096], P(('node', 'hub')), may hold values from 0 to 1023
Outputs:
- labels: float32 [32768, 128], P(('node', 'hub'))
All inputs are finite; a program needn't handle non-finite values. No bound on the sum of `seed_mask` on one device may be relied on, other than what follows from the above.
Results may differ from a plain program's by a relative error of at most 0.00041.
Values may be sent and summed in bfloat16 or wider, within the bound.
No kernel may reach another device: no remote copies, remote signals or barrier semaphores. Data moves between devices by JAX's collectives and lax.ppermute only.
A program may use at most 64 MiB of HBM per device.

v0:
```python
import jax
import jax.numpy as jnp
from jax import lax
from jax.sharding import PartitionSpec as P

BW = 2
ITERS = 3
spread_weight = 0.8


def extended_2(block, sides, width):
    for axis, dim in sides:
        count = lax.axis_size(axis)
        forward = [(i, i + 1) for i in range(count - 1)]
        backward = [(target, source) for source, target in forward]
        low = lax.ppermute(
            lax.slice_in_dim(block, block.shape[dim] - width, None, axis=dim), axis, forward
        )
        high = lax.ppermute(lax.slice_in_dim(block, 0, width, axis=dim), axis, backward)
        block = jnp.concatenate([low, block, high], axis=dim)
    return block


def band_product(extended, tiles, offsets):
    neighbour = jnp.arange(offsets.shape[0], dtype=jnp.int32)[:, None] + BW + offsets
    return jnp.einsum(
        "bkij,bkjc->bic", tiles, extended[neighbour], preferred_element_type=jnp.float32
    )


def body(seed_scores, seed_mask, band_offsets, band_tiles, hub_blocks, hub_tiles, hub_rows):
    blocks = band_offsets.shape[0]
    block_rows = band_tiles.shape[2]
    classes = seed_scores.shape[1]
    seeds = seed_mask.astype(jnp.float32)[:, None] * seed_scores.astype(jnp.float32)
    degree = jnp.sum(band_tiles, axis=(1, 3), dtype=jnp.float32) + jnp.sum(
        hub_tiles, axis=(1, 3), dtype=jnp.float32
    )
    rim_rows = BW * block_rows
    labels = seeds
    for step in range(ITERS):
        current = labels.astype(jnp.bfloat16)
        owned = current[hub_rows]
        hub_all = lax.all_gather(owned, ("node", "hub"), axis=0, tiled=True)
        hub_labels = hub_all.reshape(-1, block_rows, classes)
        hub_part = jnp.einsum(
            "bhij,bhjc->bic", hub_tiles, hub_labels[hub_blocks], preferred_element_type=jnp.float32
        )
        extended = extended_2(current, ((("node", "hub"), 0),), rim_rows)
        extended = extended.reshape(blocks + 2 * BW, block_rows, classes)
        band_part = band_product(extended, band_tiles, band_offsets)
        gathered = ((band_part + hub_part) / degree[..., None]).reshape(-1, classes)
        labels = spread_weight * gathered + (1.0 - spread_weight) * seeds
    return labels


def solution(mesh):
    placed = (
        P(("node", "hub"), None),
        P(("node", "hub")),
        P(("node", "hub"), None),
        P(("node", "hub"), None, None, None),
        P(("node", "hub"), None),
        P(("node", "hub"), None, None, None),
        P(("node", "hub")),
    )
    return jax.shard_map(
        body, mesh=mesh, in_specs=placed, out_specs=P(("node", "hub"), None), check_vma=False
    )
```

profile of v0, /device:TPU:0, one launch (start us, length us, event | category | flops | bytes accessed | tf_op | source)
XLA Modules:
  0.0 200.4 jit_solution(5771182381775568991)
XLA Ops:
  6.5 0.8 convert_element_type.21
  8.0 1.1 fusion.12
  9.2 1.3 gather_fusion.1
  10.6 4.9 %collective-permute-start = (bf16[256,128]{1,0:T(8,128)(2,1)S(1)}, bf16[256,128]{1,0:T(8,128)(2,1)S(1)}, u32[]{:S(2)}, u32[]{:S(2)}) collective-permute-start(bf16[256,128]{1,0:T(8,128)(2,1)S(1)} %get-tuple-element.9), channel_id=1, source_target_pairs={{0,1},{1,2},{2,3},{3,4},{4,5},{5,6},{6,7},{7,8},{8,9},{9,10},{10,1... | collective-permute-start | bytes 196616 | tf_op jit(solution)/shard_map/ppermute | solution.py:16
  15.5 1.3 collective-permute-start.1
  16.9 0.8 compare_select_fusion.1
  18.5 1.7 convert_reduce_fusion.1
  21.2 0.7 collective-permute-done.1
  21.9 2.5 %gather_fusion = bf16[80,128,128]{2,1,0:T(8,128)(2,1)} fusion(bf16[12,128,128]{2,1,0:T(8,128)(2,1)S(1)} %bitcast.77, s32[1024]{0:T(1024)S(1)} %pad_clamp_fusion.2), kind=kCustom, calls=%fused_computation | custom fusion | bytes 5243200 | tf_op jit(solution)/shard_map/gather | solution.py:27
  24.5 2.6 %convolution_bitcast_fusion.5 = f32[8,128,128]{1,2,0:T(8,128)S(1)} fusion(bf16[8,10,128,128]{3,2,1,0:T(8,128)(2,1)S(1)} %copy-done, bf16[8,10,128,128]{3,2,1,0:T(8,128)(2,1)} %bitcast.80), kind=kOutput, calls=%fused_computation.16 | convolution fusion | flops 335544320 | bytes 5767168 | tf_op jit(solution)/shard_map/bkij,bkjc->bic/dot_general | solution.py:26
  27.1 40.1 %all-gather.7.cloned.1.call-done = bf16[4096,128]{1,0:T(8,128)(2,1)} async-done(((bf16[128,128]{1,0:T(8,128)(2,1)}), bf16[4096,128]{1,0:T(8,128)(2,1)}) %all-gather.7.cloned.1.call-update) | async-done | bytes 1048592 | tf_op jit(solution)/shard_map/all_gather | solution.py:44
  67.1 3.2 %gather_fusion.2 = bf16[48,128,128]{2,1,0:T(8,128)(2,1)} fusion(bf16[32,128,128]{2,1,0:T(8,128)(2,1)} %bitcast.82, s32[1024]{0:T(1024)S(1)} %pad_clamp_fusion), kind=kCustom, calls=%fused_computation.2 | custom fusion | bytes 3145920 | tf_op jit(solution)/shard_map/gather | solution.py:47
  70.3 2.5 %fusion.2 = f32[8,128,128]{1,2,0:T(8,128)S(1)} fusion(f32[8,128,128]{1,2,0:T(8,128)S(1)} %convolution_bitcast_fusion.5, bf16[8,6,128,128]{3,2,1,0:T(8,128)(2,1)} %param.12, bf16[8,6,128,128]{3,2,1,0:T(8,128)(2,1)} %bitcast.86, f32[8,128]{1,0:T(8,128)S(1)} %copy-done.3), kind=kOutput, calls=%fused_computation.19 | convolution fusion | flops 201719808 | bytes 4198400 | tf_op jit(solution)/shard_map/bhij,bhjc->bic/dot_general | solution.py:46
  73.1 1.3 gather_fusion.4
  74.5 2.6 %collective-permute-start.2 = (bf16[256,128]{1,0:T(8,128)(2,1)S(1)}, bf16[256,128]{1,0:T(8,128)(2,1)S(1)}, u32[]{:S(2)}, u32[]{:S(2)}) collective-permute-start(bf16[256,128]{1,0:T(8,128)(2,1)S(1)} %get-tuple-element.7), channel_id=1, source_target_pairs={{0,1},{1,2},{2,3},{3,4},{4,5},{5,6},{6,7},{7,8},{8,9},{9,10},{10,1... | collective-permute-start | bytes 196616 | tf_op jit(solution)/shard_map/ppermute | solution.py:16
  77.1 1.3 collective-permute-start.3
  79.0 5.4 %collective-permute-done.3 = bf16[256,128]{1,0:T(8,128)(2,1)S(1)} collective-permute-done((bf16[256,128]{1,0:T(8,128)(2,1)S(1)}, bf16[256,128]{1,0:T(8,128)(2,1)S(1)}, u32[]{:S(2)}, u32[]{:S(2)}) %collective-permute-start.3) | collective-permute-done | bytes 65568 | tf_op jit(solution)/shard_map/ppermute | solution.py:19
  84.5 2.5 %gather_fusion.3 = bf16[80,128,128]{2,1,0:T(8,128)(2,1)} fusion(bf16[12,128,128]{2,1,0:T(8,128)(2,1)S(1)} %bitcast.78, s32[1024]{0:T(1024)S(1)} %pad_clamp_fusion.2), kind=kCustom, calls=%fused_computation.3 | custom fusion | bytes 5243200 | tf_op jit(solution)/shard_map/gather | solution.py:27
  87.0 2.6 %convolution_bitcast_fusion.3 = f32[8,128,128]{1,2,0:T(8,128)S(1)} fusion(bf16[8,10,128,128]{3,2,1,0:T(8,128)(2,1)S(1)} %copy-done, bf16[8,10,128,128]{3,2,1,0:T(8,128)(2,1)} %bitcast.81), kind=kOutput, calls=%fused_computation.14 | convolution fusion | flops 335544320 | bytes 5767168 | tf_op jit(solution)/shard_map/bkij,bkjc->bic/dot_general | solution.py:26
  89.6 37.8 %all-gather.9.cloned.1.call-done = bf16[4096,128]{1,0:T(8,128)(2,1)} async-done(((bf16[128,128]{1,0:T(8,128)(2,1)}), bf16[4096,128]{1,0:T(8,128)(2,1)}) %all-gather.9.cloned.1.call-update) | async-done | bytes 1048592 | tf_op jit(solution)/shard_map/all_gather | solution.py:44
  127.4 3.2 %gather_fusion.5 = bf16[48,128,128]{2,1,0:T(8,128)(2,1)} fusion(bf16[32,128,128]{2,1,0:T(8,128)(2,1)} %bitcast.83, s32[1024]{0:T(1024)S(1)} %pad_clamp_fusion), kind=kCustom, calls=%fused_computation.5 | custom fusion | bytes 3145920 | tf_op jit(solution)/shard_map/gather | solution.py:47
  130.6 2.5 %fusion.5 = f32[8,128,128]{1,2,0:T(8,128)S(1)} fusion(f32[8,128,128]{1,2,0:T(8,128)S(1)} %convolution_bitcast_fusion.3, bf16[8,6,128,128]{3,2,1,0:T(8,128)(2,1)} %param.12, bf16[8,6,128,128]{3,2,1,0:T(8,128)(2,1)} %bitcast.87, f32[8,128]{1,0:T(8,128)S(1)} %copy-done.4), kind=kOutput, calls=%fused_computation.22 | convolution fusion | flops 201719808 | bytes 4198400 | tf_op jit(solution)/shard_map/bhij,bhjc->bic/dot_general | solution.py:46
  133.3 1.3 gather_fusion.7
  134.6 2.6 %collective-permute-start.4 = (bf16[256,128]{1,0:T(8,128)(2,1)S(1)}, bf16[256,128]{1,0:T(8,128)(2,1)S(1)}, u32[]{:S(2)}, u32[]{:S(2)}) collective-permute-start(bf16[256,128]{1,0:T(8,128)(2,1)S(1)} %get-tuple-element.5), channel_id=1, source_target_pairs={{0,1},{1,2},{2,3},{3,4},{4,5},{5,6},{6,7},{7,8},{8,9},{9,10},{10,1... | collective-permute-start | bytes 196616 | tf_op jit(solution)/shard_map/ppermute | solution.py:16
  137.3 1.3 collective-permute-start.5
  139.2 5.4 %collective-permute-done.5 = bf16[256,128]{1,0:T(8,128)(2,1)S(1)} collective-permute-done((bf16[256,128]{1,0:T(8,128)(2,1)S(1)}, bf16[256,128]{1,0:T(8,128)(2,1)S(1)}, u32[]{:S(2)}, u32[]{:S(2)}) %collective-permute-start.5) | collective-permute-done | bytes 65568 | tf_op jit(solution)/shard_map/ppermute | solution.py:19
  144.6 2.5 %gather_fusion.6 = bf16[80,128,128]{2,1,0:T(8,128)(2,1)} fusion(bf16[12,128,128]{2,1,0:T(8,128)(2,1)S(1)} %bitcast.76, s32[1024]{0:T(1024)S(1)} %pad_clamp_fusion.2), kind=kCustom, calls=%fused_computation.6 | custom fusion | bytes 5243200 | tf_op jit(solution)/shard_map/gather | solution.py:27
  147.2 2.6 %convolution_bitcast_fusion.1 = f32[8,128,128]{1,2,0:T(8,128)S(1)} fusion(bf16[8,10,128,128]{3,2,1,0:T(8,128)(2,1)S(1)} %copy-done, bf16[8,10,128,128]{3,2,1,0:T(8,128)(2,1)} %bitcast.79), kind=kOutput, calls=%fused_computation.12 | convolution fusion | flops 335544320 | bytes 5767168 | tf_op jit(solution)/shard_map/bkij,bkjc->bic/dot_general | solution.py:26
  149.7 37.9 %all-gather.11.cloned.1.call-done = bf16[4096,128]{1,0:T(8,128)(2,1)} async-done(((bf16[128,128]{1,0:T(8,128)(2,1)}), bf16[4096,128]{1,0:T(8,128)(2,1)}) %all-gather.11.cloned.1.call-update) | async-done | bytes 1048592 | tf_op jit(solution)/shard_map/all_gather | solution.py:44
  187.6 3.2 %gather_fusion.8 = bf16[48,128,128]{2,1,0:T(8,128)(2,1)} fusion(bf16[32,128,128]{2,1,0:T(8,128)(2,1)} %bitcast.84, s32[1024]{0:T(1024)S(1)} %pad_clamp_fusion), kind=kCustom, calls=%fused_computation.8 | custom fusion | bytes 3145920 | tf_op jit(solution)/shard_map/gather | solution.py:47
  190.8 2.0 fusion.8
  192.8 1.0 bitcast_add_fusion
  (39 shorter events, 4.4 us)
Async XLA Ops:
  6.5 13.6 %copy-start = (bf16[8,10,128,128]{3,2,1,0:T(8,128)(2,1)S(1)}, bf16[8,10,128,128]{3,2,1,0:T(8,128)(2,1)}, u32[]{:S(2)}) copy-start(bf16[8,10,128,128]{3,2,1,0:T(8,128)(2,1)} %param.10) | copy-start | bytes 7864324
  6.5 60.6 %all-gather.7.cloned.1.call-start = ((), (), s32[]{:S(2)}) async-start(), calls=%async_computation | async-start | bytes 1081344 | tf_op jit(solution)/shard_map/all_gather | solution.py:44
  10.5 116.9 %all-gather.9.cloned.1.call-start = ((), (), s32[]{:S(2)}) async-start(), calls=%async_computation.1 | async-start | bytes 1081344 | tf_op jit(solution)/shard_map/all_gather | solution.py:44
  10.6 10.6 %collective-permute-start = (bf16[256,128]{1,0:T(8,128)(2,1)S(1)}, bf16[256,128]{1,0:T(8,128)(2,1)S(1)}, u32[]{:S(2)}, u32[]{:S(2)}) collective-permute-start(bf16[256,128]{1,0:T(8,128)(2,1)S(1)} %get-tuple-element.9), channel_id=1, source_target_pairs={{0,1},{1,2},{2,3},{3,4},{4,5},{5,6},{6,7},{7,8},{8,9},{9,10},{10,1... | collective-permute-start | bytes 196616 | tf_op jit(solution)/shard_map/ppermute | solution.py:16
  15.5 6.4 %collective-permute-start.1 = (bf16[256,128]{1,0:T(8,128)(2,1)S(1)}, bf16[256,128]{1,0:T(8,128)(2,1)S(1)}, u32[]{:S(2)}, u32[]{:S(2)}) collective-permute-start(bf16[256,128]{1,0:T(8,128)(2,1)S(1)} %get-tuple-element.10), channel_id=1, source_target_pairs={{1,0},{2,1},{3,2},{4,3},{5,4},{6,5},{7,6},{8,7},{9,8},{10,9},{11,1... | collective-permute-start | bytes 196616 | tf_op jit(solution)/shard_map/ppermute | solution.py:19
  27.0 43.3 %copy-start.3 = (f32[8,128]{1,0:T(8,128)S(1)}, f32[8,128]{1,0:T(8,128)}, u32[]{:S(2)}) copy-start(f32[8,128]{1,0:T(8,128)} %add.76) | copy-start | bytes 12292
  70.3 2.5 %copy-start.1 = (bf16[1024,128]{1,0:T(8,128)(2,1)S(1)}, bf16[1024,128]{1,0:T(8,128)(2,1)}, u32[]{:S(2)}) copy-start(bf16[1024,128]{1,0:T(8,128)(2,1)} %param.7) | copy-start | bytes 786436
  74.4 113.2 %all-gather.11.cloned.1.call-start = ((), (), s32[]{:S(2)}) async-start(), calls=%async_computation.2 | async-start | bytes 1081344 | tf_op jit(solution)/shard_map/all_gather | solution.py:44
  74.5 4.5 %collective-permute-start.2 = (bf16[256,128]{1,0:T(8,128)(2,1)S(1)}, bf16[256,128]{1,0:T(8,128)(2,1)S(1)}, u32[]{:S(2)}, u32[]{:S(2)}) collective-permute-start(bf16[256,128]{1,0:T(8,128)(2,1)S(1)} %get-tuple-element.7), channel_id=1, source_target_pairs={{0,1},{1,2},{2,3},{3,4},{4,5},{5,6},{6,7},{7,8},{8,9},{9,10},{10,1... | collective-permute-start | bytes 196616 | tf_op jit(solution)/shard_map/ppermute | solution.py:16
  77.1 7.3 %collective-permute-start.3 = (bf16[256,128]{1,0:T(8,128)(2,1)S(1)}, bf16[256,128]{1,0:T(8,128)(2,1)S(1)}, u32[]{:S(2)}, u32[]{:S(2)}) collective-permute-start(bf16[256,128]{1,0:T(8,128)(2,1)S(1)} %get-tuple-element.8), channel_id=1, source_target_pairs={{1,0},{2,1},{3,2},{4,3},{5,4},{6,5},{7,6},{8,7},{9,8},{10,9},{11,1... | collective-permute-start | bytes 196616 | tf_op jit(solution)/shard_map/ppermute | solution.py:19
  89.6 41.0 %copy-start.4 = (f32[8,128]{1,0:T(8,128)S(1)}, f32[8,128]{1,0:T(8,128)}, u32[]{:S(2)}) copy-start(f32[8,128]{1,0:T(8,128)} %add.76) | copy-start | bytes 12292
  134.6 4.5 %collective-permute-start.4 = (bf16[256,128]{1,0:T(8,128)(2,1)S(1)}, bf16[256,128]{1,0:T(8,128)(2,1)S(1)}, u32[]{:S(2)}, u32[]{:S(2)}) collective-permute-start(bf16[256,128]{1,0:T(8,128)(2,1)S(1)} %get-tuple-element.5), channel_id=1, source_target_pairs={{0,1},{1,2},{2,3},{3,4},{4,5},{5,6},{6,7},{7,8},{8,9},{9,10},{10,1... | collective-permute-start | bytes 196616 | tf_op jit(solution)/shard_map/ppermute | solution.py:16
  137.3 7.3 %collective-permute-start.5 = (bf16[256,128]{1,0:T(8,128)(2,1)S(1)}, bf16[256,128]{1,0:T(8,128)(2,1)S(1)}, u32[]{:S(2)}, u32[]{:S(2)}) collective-permute-start(bf16[256,128]{1,0:T(8,128)(2,1)S(1)} %get-tuple-element.6), channel_id=1, source_target_pairs={{1,0},{2,1},{3,2},{4,3},{5,4},{6,5},{7,6},{8,7},{9,8},{10,9},{11,1... | collective-permute-start | bytes 196616 | tf_op jit(solution)/shard_map/ppermute | solution.py:19
  149.7 41.1 %copy-start.2 = (bf16[8,6,128,128]{3,2,1,0:T(8,128)(2,1)S(1)}, bf16[8,6,128,128]{3,2,1,0:T(8,128)(2,1)}, u32[]{:S(2)}) copy-start(bf16[8,6,128,128]{3,2,1,0:T(8,128)(2,1)} %param.12) | copy-start | bytes 4718596
  149.7 41.1 %copy-start.5 = (f32[8,128]{1,0:T(8,128)S(1)}, f32[8,128]{1,0:T(8,128)}, u32[]{:S(2)}) copy-start(f32[8,128]{1,0:T(8,128)} %add.76) | copy-start | bytes 12292
Sparse Core Ops, SparseCore 0:
  10.7 56.4 all-gather.6
  74.5 52.8 all-gather.8
  134.7 52.8 all-gather.10
where the time goes:
time: 201 us; the launch traced here: 200 us
  waiting for transfers between devices  129 us (64%)
  local copies, waits for them, and re-layouts  21.4 us (11%)
  matrix products  14.7 us (7%)
  starting transfers between devices  14.2 us (7%)
  between operations  13.3 us (7%)
  other arithmetic  8.3 us (4%)
    all_gather x3, waiting for transfers between devices, body(): hub_all = lax.all_gather(owned, ('node', 'hub'), axis=0, tiled=True)  116 us
    ppermute x3, waiting for transfers between devices, extended_2(): lax.ppermute(lax.slice_in_dim(block, 0, width, axis=dim), axis, backward)  11.5 us
    ppermute x3, starting transfers between devices, extended_2(): lax.ppermute(lax.slice_in_dim(block, block.shape[dim] - width, None, axis...  10.2 us
    gather x3, local copies, waits for them, and re-layouts, body(): hub_labels[hub_blocks]  9.58 us
    dot_general x3, matrix products, band_product(): jnp.einsum('bkij,bkjc->bic', tiles, extended[neighbour], preferred_elemen...  7.72 us
    gather x3, local copies, waits for them, and re-layouts, band_product(): extended[neighbour]  7.61 us
    dot_general x3, matrix products, body(): jnp.einsum('bhij,bhjc->bic', hub_tiles, hub_labels[hub_blocks], preferred...  6.95 us
  transfers between devices with their start and end apart: 9, of which 8 were waited for; matrix products, arithmetic and copies ran while one was open for 10% of the time, Pallas kernels for 0%

commit v1 on v0

--- a/solution.py
+++ b/solution.py
@@ -6,6 +6,24 @@
 BW = 2
 ITERS = 3
 spread_weight = 0.8
+
+
+def laid_out(parts, dim):
+    parts = jnp.moveaxis(parts, 0, dim)
+    shape = parts.shape
+    return parts.reshape(*shape[:dim], shape[dim] * shape[dim + 1], *shape[dim + 2 :])
+
+
+def collected_by_bits(x, axis):
+    length = lax.axis_size(axis)
+    tiles = x[None]
+    for level in range(length.bit_length() - 1):
+        stride = 1 << level
+        other = lax.ppermute(tiles, axis, [(i, i ^ stride) for i in range(length)])
+        both = jnp.stack([tiles, other])
+        upper = lax.axis_index(axis) >> level & 1
+        tiles = jnp.where(upper == 0, both, both[::-1]).reshape(-1, *x.shape)
+    return tiles
 
 
 def extended_2(block, sides, width):
@@ -41,7 +59,7 @@
     for step in range(ITERS):
         current = labels.astype(jnp.bfloat16)
         owned = current[hub_rows]
-        hub_all = lax.all_gather(owned, ("node", "hub"), axis=0, tiled=True)
+        hub_all = laid_out(collected_by_bits(owned, ("node", "hub")), 0)
         hub_labels = hub_all.reshape(-1, block_rows, classes)
         hub_part = jnp.einsum(
             "bhij,bhjc->bic", hub_tiles, hub_labels[hub_blocks], preferred_element_type=jnp.float32

time: 201 us -> 143 us (0.71)
  waiting for transfers between devices: 129 us -> 47.5 us
  starting transfers between devices: 14.2 us -> 42.3 us
  between operations: 13.3 us -> 0.42 us
  other arithmetic: 8.3 us -> 16.2 us
  local copies, waits for them, and re-layouts: 21.4 us -> 18.5 us
  matrix products: 14.7 us -> 17.4 us
    all_gather x3 -> x0, waiting for transfers between devices: 116 us -> none  [body(): hub_all = lax.all_gather(owned, ('node', 'hub'), axis=0, tiled=True)]
    ppermute x0 -> x15, waiting for transfers between devices: none -> 47.5 us  [collected_by_bits(): other = lax.ppermute(tiles, axis, [(i, i ^ stride) for i in range(length)])]
    ppermute x0 -> x15, starting transfers between devices: none -> 23.5 us  [collected_by_bits(): other = lax.ppermute(tiles, axis, [(i, i ^ stride) for i in range(length)])]
    ppermute x3, waiting for transfers between devices: 11.5 us -> 0.01 us  [extended_2(): lax.ppermute(lax.slice_in_dim(block, 0, width, axis=dim), axis, backward)]
    select_n x0 -> x12, other arithmetic: none -> 5 us  [collected_by_bits(): tiles = jnp.where(upper == 0, both, both[::-1]).reshape(-1, *x.shape)]
    ppermute x3, starting transfers between devices: 10.2 us -> 14.8 us  [extended_2(): lax.ppermute(lax.slice_in_dim(block, block.shape[dim] - width, None, axis...]
    another operation x0 -> x18, other arithmetic: none -> 4.09 us  [collected_by_bits(): both = jnp.stack([tiles, other])]
    dot_general x3, matrix products: 7.72 us -> 10.1 us  [band_product(): jnp.einsum('bkij,bkjc->bic', tiles, extended[neighbour], preferred_elemen...]
  transfers between devices with their start and end apart: 9 -> 21, of which waited for: 8 -> 14; matrix products, arithmetic and copies ran while one was open for 10% -> 17% of each run, Pallas kernels for 0% -> 0%
where the time goes in v1:
time: 143 us; the launch traced here: 142 us
  waiting for transfers between devices  47.5 us (33%)
  starting transfers between devices  42.3 us (30%)
  local copies, waits for them, and re-layouts  18.5 us (13%)
  matrix products  17.4 us (12%)
  other arithmetic  16.2 us (11%)
    ppermute x15, waiting for transfers between devices, collected_by_bits(): other = lax.ppermute(tiles, axis, [(i, i ^ stride) for i in range(length)])  47.5 us
    ppermute x15, starting transfers between devices, collected_by_bits(): other = lax.ppermute(tiles, axis, [(i, i ^ stride) for i in range(length)])  23.5 us
    ppermute x3, starting transfers between devices, extended_2(): lax.ppermute(lax.slice_in_dim(block, block.shape[dim] - width, None, axis...  14.8 us
    dot_general x3, matrix products, band_product(): jnp.einsum('bkij,bkjc->bic', tiles, extended[neighbour], preferred_elemen...  10.1 us
    gather x3, local copies, waits for them, and re-layouts, body(): hub_labels[hub_blocks]  8.44 us
    gather x3, local copies, waits for them, and re-layouts, band_product(): extended[neighbour]  7.65 us
    dot_general x3, matrix products, body(): jnp.einsum('bhij,bhjc->bic', hub_tiles, hub_labels[hub_blocks], preferred...  7.27 us
    select_n x12, other arithmetic, collected_by_bits(): tiles = jnp.where(upper == 0, both, both[::-1]).reshape(-1, *x.shape)  5 us
  transfers between devices with their start and end apart: 21, of which 14 were waited for; matrix products, arithmetic and copies ran while one was open for 17% of the time, Pallas kernels for 0%

profile of v1, /device:TPU:0, one launch (start us, length us, event | category | flops | bytes accessed | tf_op | source)
XLA Modules:
  0.0 142.3 jit_solution(15565831166100399525)
XLA Ops:
  3.3 5.6 %collective-permute-start = (bf16[256,128]{1,0:T(8,128)(2,1)S(1)}, bf16[256,128]{1,0:T(8,128)(2,1)S(1)}, u32[]{:S(2)}, u32[]{:S(2)}) collective-permute-start(bf16[256,128]{1,0:T(8,128)(2,1)S(1)} %get-tuple-element.9), channel_id=1, source_target_pairs={{0,1},{1,2},{2,3},{3,4},{4,5},{5,6},{6,7},{7,8},{8,9},{9,10},{10,1... | collective-permute-start | bytes 196616 | tf_op jit(solution)/shard_map/ppermute | solution.py:34
  10.3 2.1 %collective-permute-start.2 = (bf16[1,128,128]{2,1,0:T(8,128)(2,1)S(1)}, bf16[1,128,128]{2,1,0:T(8,128)(2,1)S(1)}, u32[]{:S(2)}, u32[]{:S(2)}) collective-permute-start(bf16[1,128,128]{2,1,0:T(8,128)(2,1)S(1)} %bitcast.162), channel_id=1, source_target_pairs={{0,1},{1,0},{2,3},{3,2},{4,5},{5,4},{6,7},{7,6},{8,9},{9,8},{10,11... | collective-permute-start | bytes 98312 | tf_op jit(solution)/shard_map/ppermute | solution.py:22
  12.4 2.2 %convert_reduce_fusion = f32[8,128]{1,0:T(8,128)S(1)} fusion(bf16[8,10,128,128]{3,2,1,0:T(8,128)(2,1)} %param.10), kind=kLoop, calls=%fused_computation.9 | loop fusion | flops 2620416 | bytes 2625536 | tf_op jit(solution)/shard_map/reduce_sum | solution.py:54
  14.6 4.2 %collective-permute-start.3 = (bf16[2,128,128]{2,1,0:T(8,128)(2,1)S(1)}, bf16[2,128,128]{2,1,0:T(8,128)(2,1)S(1)}, u32[]{:S(2)}, u32[]{:S(2)}) collective-permute-start(bf16[2,128,128]{2,1,0:T(8,128)(2,1)S(1)} %get-tuple-element.16), channel_id=1, source_target_pairs={{0,2},{1,3},{2,0},{3,1},{4,6},{5,7},{6,4},{7,5},{8,10},{9,11},{10,... | collective-permute-start | bytes 196616 | tf_op jit(solution)/shard_map/ppermute | solution.py:22
  18.8 4.0 %collective-permute-done.3 = bf16[2,128,128]{2,1,0:T(8,128)(2,1)S(1)} collective-permute-done((bf16[2,128,128]{2,1,0:T(8,128)(2,1)S(1)}, bf16[2,128,128]{2,1,0:T(8,128)(2,1)S(1)}, u32[]{:S(2)}, u32[]{:S(2)}) %collective-permute-start.3) | collective-permute-done | bytes 65568 | tf_op jit(solution)/shard_map/ppermute | solution.py:22
  26.8 6.1 %collective-permute-done.5 = bf16[8,128,128]{2,1,0:T(8,128)(2,1)S(1)} collective-permute-done((bf16[8,128,128]{2,1,0:T(8,128)(2,1)S(1)}, bf16[8,128,128]{2,1,0:T(8,128)(2,1)S(1)}, u32[]{:S(2)}, u32[]{:S(2)}) %collective-permute-start.5) | collective-permute-done | bytes 262176 | tf_op jit(solution)/shard_map/ppermute | solution.py:22
  34.8 2.6 %gather_fusion = bf16[80,128,128]{2,1,0:T(8,128)(2,1)} fusion(bf16[12,128,128]{2,1,0:T(8,128)(2,1)S(1)} %bitcast.134, s32[1024]{0:T(1024)S(1)} %pad_clamp_fusion.2), kind=kCustom, calls=%fused_computation | custom fusion | bytes 5243200 | tf_op jit(solution)/shard_map/gather | solution.py:45
  37.4 3.4 %convolution_bitcast_fusion.5 = f32[8,128,128]{1,2,0:T(8,128)} fusion(bf16[8,10,128,128]{3,2,1,0:T(8,128)(2,1)S(1)} %copy-done, bf16[8,10,128,128]{3,2,1,0:T(8,128)(2,1)} %bitcast.137), kind=kOutput, calls=%fused_computation.19 | convolution fusion | flops 335544320 | bytes 5767168 | tf_op jit(solution)/shard_map/bkij,bkjc->bic/dot_general | solution.py:44
  40.7 5.6 %collective-permute-done.6 = bf16[16,128,128]{2,1,0:T(8,128)(2,1)} collective-permute-done((bf16[16,128,128]{2,1,0:T(8,128)(2,1)S(1)}, bf16[16,128,128]{2,1,0:T(8,128)(2,1)}, u32[]{:S(2)}, u32[]{:S(2)}) %collective-permute-start.6) | collective-permute-done | bytes 524320 | tf_op jit(solution)/shard_map/ppermute | solution.py:22
  48.8 3.2 %gather_fusion.2 = bf16[48,128,128]{2,1,0:T(8,128)(2,1)} fusion(bf16[32,128,128]{2,1,0:T(8,128)(2,1)} %bitcast.140, s32[1024]{0:T(1024)S(1)} %pad_clamp_fusion), kind=kCustom, calls=%fused_computation.2 | custom fusion | bytes 3145920 | tf_op jit(solution)/shard_map/gather | solution.py:65
  52.0 2.6 %fusion.2 = f32[8,128,128]{1,2,0:T(8,128)S(1)} fusion(f32[8,128,128]{1,2,0:T(8,128)} %convolution_bitcast_fusion.5, bf16[8,6,128,128]{3,2,1,0:T(8,128)(2,1)} %param.12, bf16[8,6,128,128]{3,2,1,0:T(8,128)(2,1)} %bitcast.145, f32[8,128]{1,0:T(8,128)S(1)} %copy-done.4), kind=kOutput, calls=%fused_computation.22 | convolution fusion | flops 201719808 | bytes 4198400 | tf_op jit(solution)/shard_map/bhij,bhjc->bic/dot_general | solution.py:64
  56.6 2.9 %collective-permute-done.9 = bf16[1,128,128]{2,1,0:T(8,128)(2,1)S(1)} collective-permute-done((bf16[1,128,128]{2,1,0:T(8,128)(2,1)S(1)}, bf16[1,128,128]{2,1,0:T(8,128)(2,1)S(1)}, u32[]{:S(2)}, u32[]{:S(2)}) %collective-permute-start.9) | collective-permute-done | bytes 32800 | tf_op jit(solution)/shard_map/ppermute | solution.py:22
  59.6 2.5 %collective-permute-start.10 = (bf16[2,128,128]{2,1,0:T(8,128)(2,1)S(1)}, bf16[2,128,128]{2,1,0:T(8,128)(2,1)S(1)}, u32[]{:S(2)}, u32[]{:S(2)}) collective-permute-start(bf16[2,128,128]{2,1,0:T(8,128)(2,1)S(1)} %get-tuple-element.14), channel_id=1, source_target_pairs={{0,2},{1,3},{2,0},{3,1},{4,6},{5,7},{6,4},{7,5},{8,10},{9,11},{10,... | collective-permute-start | bytes 196616 | tf_op jit(solution)/shard_map/ppermute | solution.py:22
  62.0 2.8 %collective-permute-done.10 = bf16[2,128,128]{2,1,0:T(8,128)(2,1)S(1)} collective-permute-done((bf16[2,128,128]{2,1,0:T(8,128)(2,1)S(1)}, bf16[2,128,128]{2,1,0:T(8,128)(2,1)S(1)}, u32[]{:S(2)}, u32[]{:S(2)}) %collective-permute-start.10) | collective-permute-done | bytes 65568 | tf_op jit(solution)/shard_map/ppermute | solution.py:22
  66.4 1.7 %collective-permute-start.12 = (bf16[8,128,128]{2,1,0:T(8,128)(2,1)S(1)}, bf16[8,128,128]{2,1,0:T(8,128)(2,1)S(1)}, u32[]{:S(2)}, u32[]{:S(2)}) collective-permute-start(bf16[8,128,128]{2,1,0:T(8,128)(2,1)S(1)} %bitcast.151), channel_id=1, source_target_pairs={{0,8},{1,9},{2,10},{3,11},{4,12},{5,13},{6,14},{7,15},{8,0},{9,1},... | collective-permute-start | bytes 786440 | tf_op jit(solution)/shard_map/ppermute | solution.py:22
  69.4 4.5 %collective-permute-start.7 = (bf16[256,128]{1,0:T(8,128)(2,1)S(1)}, bf16[256,128]{1,0:T(8,128)(2,1)S(1)}, u32[]{:S(2)}, u32[]{:S(2)}) collective-permute-start(bf16[256,128]{1,0:T(8,128)(2,1)S(1)} %get-tuple-element.7), channel_id=1, source_target_pairs={{0,1},{1,2},{2,3},{3,4},{4,5},{5,6},{6,7},{7,8},{8,9},{9,10},{10,1... | collective-permute-start | bytes 196616 | tf_op jit(solution)/shard_map/ppermute | solution.py:34
  75.7 2.4 %collective-permute-start.13 = (bf16[16,128,128]{2,1,0:T(8,128)(2,1)}, bf16[16,128,128]{2,1,0:T(8,128)(2,1)}, u32[]{:S(2)}, u32[]{:S(2)}) collective-permute-start(bf16[16,128,128]{2,1,0:T(8,128)(2,1)} %bitcast.43), channel_id=1, source_target_pairs={{0,16},{1,17},{2,18},{3,19},{4,20},{5,21},{6,22},{7,23},{8,24},{9,... | collective-permute-start | bytes 1572872 | tf_op jit(solution)/shard_map/ppermute | solution.py:22
  78.1 2.6 %gather_fusion.3 = bf16[80,128,128]{2,1,0:T(8,128)(2,1)} fusion(bf16[12,128,128]{2,1,0:T(8,128)(2,1)S(1)} %bitcast.135, s32[1024]{0:T(1024)S(1)} %pad_clamp_fusion.2), kind=kCustom, calls=%fused_computation.3 | custom fusion | bytes 5243200 | tf_op jit(solution)/shard_map/gather | solution.py:45
  80.7 3.4 %convolution_bitcast_fusion.3 = f32[8,128,128]{1,2,0:T(8,128)} fusion(bf16[8,10,128,128]{3,2,1,0:T(8,128)(2,1)S(1)} %copy-done, bf16[8,10,128,128]{3,2,1,0:T(8,128)(2,1)} %bitcast.138), kind=kOutput, calls=%fused_computation.17 | convolution fusion | flops 335544320 | bytes 5767168 | tf_op jit(solution)/shard_map/bkij,bkjc->bic/dot_general | solution.py:44
  84.1 6.9 %collective-permute-done.13 = bf16[16,128,128]{2,1,0:T(8,128)(2,1)} collective-permute-done((bf16[16,128,128]{2,1,0:T(8,128)(2,1)}, bf16[16,128,128]{2,1,0:T(8,128)(2,1)}, u32[]{:S(2)}, u32[]{:S(2)}) %collective-permute-start.13) | collective-permute-done | bytes 524320 | tf_op jit(solution)/shard_map/ppermute | solution.py:22
  93.5 3.2 %gather_fusion.5 = bf16[48,128,128]{2,1,0:T(8,128)(2,1)} fusion(bf16[32,128,128]{2,1,0:T(8,128)(2,1)} %bitcast.141, s32[1024]{0:T(1024)S(1)} %pad_clamp_fusion), kind=kCustom, calls=%fused_computation.5 | custom fusion | bytes 3145920 | tf_op jit(solution)/shard_map/gather | solution.py:65
  96.8 2.6 %fusion.5 = f32[8,128,128]{1,2,0:T(8,128)S(1)} fusion(f32[8,128,128]{1,2,0:T(8,128)} %convolution_bitcast_fusion.3, bf16[8,6,128,128]{3,2,1,0:T(8,128)(2,1)} %param.12, bf16[8,6,128,128]{3,2,1,0:T(8,128)(2,1)} %bitcast.146, f32[8,128]{1,0:T(8,128)S(1)} %copy-done.5), kind=kOutput, calls=%fused_computation.25 | convolution fusion | flops 201719808 | bytes 4198400 | tf_op jit(solution)/shard_map/bhij,bhjc->bic/dot_general | solution.py:64
  100.3 3.9 %collective-permute-done.16 = bf16[1,128,128]{2,1,0:T(8,128)(2,1)S(1)} collective-permute-done((bf16[1,128,128]{2,1,0:T(8,128)(2,1)S(1)}, bf16[1,128,128]{2,1,0:T(8,128)(2,1)S(1)}, u32[]{:S(2)}, u32[]{:S(2)}) %collective-permute-start.16) | collective-permute-done | bytes 32800 | tf_op jit(solution)/shard_map/ppermute | solution.py:22
  104.3 2.8 %collective-permute-start.17 = (bf16[2,128,128]{2,1,0:T(8,128)(2,1)S(1)}, bf16[2,128,128]{2,1,0:T(8,128)(2,1)S(1)}, u32[]{:S(2)}, u32[]{:S(2)}) collective-permute-start(bf16[2,128,128]{2,1,0:T(8,128)(2,1)S(1)} %get-tuple-element.12), channel_id=1, source_target_pairs={{0,2},{1,3},{2,0},{3,1},{4,6},{5,7},{6,4},{7,5},{8,10},{9,11},{10,... | collective-permute-start | bytes 196616 | tf_op jit(solution)/shard_map/ppermute | solution.py:22
  107.1 2.5 %collective-permute-done.17 = bf16[2,128,128]{2,1,0:T(8,128)(2,1)S(1)} collective-permute-done((bf16[2,128,128]{2,1,0:T(8,128)(2,1)S(1)}, bf16[2,128,128]{2,1,0:T(8,128)(2,1)S(1)}, u32[]{:S(2)}, u32[]{:S(2)}) %collective-permute-start.17) | collective-permute-done | bytes 65568 | tf_op jit(solution)/shard_map/ppermute | solution.py:22
  113.6 4.7 %collective-permute-start.14 = (bf16[256,128]{1,0:T(8,128)(2,1)S(1)}, bf16[256,128]{1,0:T(8,128)(2,1)S(1)}, u32[]{:S(2)}, u32[]{:S(2)}) collective-permute-start(bf16[256,128]{1,0:T(8,128)(2,1)S(1)} %get-tuple-element.5), channel_id=1, source_target_pairs={{0,1},{1,2},{2,3},{3,4},{4,5},{5,6},{6,7},{7,8},{8,9},{9,10},{10,1... | collective-permute-start | bytes 196616 | tf_op jit(solution)/shard_map/ppermute | solution.py:34
  120.5 2.4 %collective-permute-start.20 = (bf16[16,128,128]{2,1,0:T(8,128)(2,1)}, bf16[16,128,128]{2,1,0:T(8,128)(2,1)}, u32[]{:S(2)}, u32[]{:S(2)}) collective-permute-start(bf16[16,128,128]{2,1,0:T(8,128)(2,1)} %bitcast.68), channel_id=1, source_target_pairs={{0,16},{1,17},{2,18},{3,19},{4,20},{5,21},{6,22},{7,23},{8,24},{9,... | collective-permute-start | bytes 1572872 | tf_op jit(solution)/shard_map/ppermute | solution.py:22
  122.9 2.6 %gather_fusion.6 = bf16[80,128,128]{2,1,0:T(8,128)(2,1)} fusion(bf16[12,128,128]{2,1,0:T(8,128)(2,1)S(1)} %bitcast.133, s32[1024]{0:T(1024)S(1)} %pad_clamp_fusion.2), kind=kCustom, calls=%fused_computation.6 | custom fusion | bytes 5243200 | tf_op jit(solution)/shard_map/gather | solution.py:45
  125.5 3.4 %convolution_bitcast_fusion.1 = f32[8,128,128]{1,2,0:T(8,128)} fusion(bf16[8,10,128,128]{3,2,1,0:T(8,128)(2,1)S(1)} %copy-done, bf16[8,10,128,128]{3,2,1,0:T(8,128)(2,1)} %bitcast.136), kind=kOutput, calls=%fused_computation.15 | convolution fusion | flops 335544320 | bytes 5767168 | tf_op jit(solution)/shard_map/bkij,bkjc->bic/dot_general | solution.py:44
  128.8 6.8 %collective-permute-done.20 = bf16[16,128,128]{2,1,0:T(8,128)(2,1)} collective-permute-done((bf16[16,128,128]{2,1,0:T(8,128)(2,1)}, bf16[16,128,128]{2,1,0:T(8,128)(2,1)}, u32[]{:S(2)}, u32[]{:S(2)}) %collective-permute-start.20) | collective-permute-done | bytes 524320 | tf_op jit(solution)/shard_map/ppermute | solution.py:22
  137.2 2.0 %gather_fusion.8 = bf16[48,128,128]{2,1,0:T(8,128)(2,1)} fusion(bf16[32,128,128]{2,1,0:T(8,128)(2,1)S(1)} %bitcast.139, s32[1024]{0:T(1024)S(1)} %pad_clamp_fusion), kind=kCustom, calls=%fused_computation.8 | custom fusion | bytes 3145920 | tf_op jit(solution)/shard_map/gather | solution.py:65
  139.2 2.1 %fusion.8 = f32[8,128,128]{1,2,0:T(8,128)S(1)} fusion(f32[8,128,128]{1,2,0:T(8,128)} %convolution_bitcast_fusion.1, bf16[8,6,128,128]{3,2,1,0:T(8,128)(2,1)S(1)} %copy-done.3, bf16[8,6,128,128]{3,2,1,0:T(8,128)(2,1)} %bitcast.144, f32[8,128]{1,0:T(8,128)S(1)} %copy-done.6), kind=kOutput, calls=%fused_computation.28 | convolution fusion | flops 201719808 | bytes 4198400 | tf_op jit(solution)/shard_map/bhij,bhjc->bic/dot_general | solution.py:64
  (96 shorter events, 32.0 us)
Async XLA Ops:
  0.0 18.8 %copy-start.7 = (s32[8,10]{1,0:T(8,128)S(1)}, s32[8,10]{1,0:T(8,128)}, u32[]{:S(2)}) copy-start(s32[8,10]{1,0:T(8,128)} %param.9) | copy-start | bytes 964
  0.0 23.0 %copy-start.8 = (s32[8,6]{1,0:T(8,128)S(1)}, s32[8,6]{1,0:T(8,128)}, u32[]{:S(2)}) copy-start(s32[8,6]{1,0:T(8,128)} %param.11) | copy-start | bytes 580
  1.9 23.9 %copy-start.2 = (bf16[8,6,128,128]{3,2,1,0:T(8,128)(2,1)S(1)}, bf16[8,6,128,128]{3,2,1,0:T(8,128)(2,1)}, u32[]{:S(2)}) copy-start(bf16[8,6,128,128]{3,2,1,0:T(8,128)(2,1)} %param.12) | copy-start | bytes 4718596
  1.9 32.9 %collective-permute-start.1 = (bf16[256,128]{1,0:T(8,128)(2,1)S(1)}, bf16[256,128]{1,0:T(8,128)(2,1)S(1)}, u32[]{:S(2)}, u32[]{:S(2)}) collective-permute-start(bf16[256,128]{1,0:T(8,128)(2,1)S(1)} %get-tuple-element.10), channel_id=1, source_target_pairs={{1,0},{2,1},{3,2},{4,3},{5,4},{6,5},{7,6},{8,7},{9,8},{10,9},{11,1... | collective-permute-start | bytes 196616 | tf_op jit(solution)/shard_map/ppermute | solution.py:37
  3.3 31.4 %collective-permute-start = (bf16[256,128]{1,0:T(8,128)(2,1)S(1)}, bf16[256,128]{1,0:T(8,128)(2,1)S(1)}, u32[]{:S(2)}, u32[]{:S(2)}) collective-permute-start(bf16[256,128]{1,0:T(8,128)(2,1)S(1)} %get-tuple-element.9), channel_id=1, source_target_pairs={{0,1},{1,2},{2,3},{3,4},{4,5},{5,6},{6,7},{7,8},{8,9},{9,10},{10,1... | collective-permute-start | bytes 196616 | tf_op jit(solution)/shard_map/ppermute | solution.py:34
  10.3 4.2 %collective-permute-start.2 = (bf16[1,128,128]{2,1,0:T(8,128)(2,1)S(1)}, bf16[1,128,128]{2,1,0:T(8,128)(2,1)S(1)}, u32[]{:S(2)}, u32[]{:S(2)}) collective-permute-start(bf16[1,128,128]{2,1,0:T(8,128)(2,1)S(1)} %bitcast.162), channel_id=1, source_target_pairs={{0,1},{1,0},{2,3},{3,2},{4,5},{5,4},{6,7},{7,6},{8,9},{9,8},{10,11... | collective-permute-start | bytes 98312 | tf_op jit(solution)/shard_map/ppermute | solution.py:22
  14.6 8.3 %collective-permute-start.3 = (bf16[2,128,128]{2,1,0:T(8,128)(2,1)S(1)}, bf16[2,128,128]{2,1,0:T(8,128)(2,1)S(1)}, u32[]{:S(2)}, u32[]{:S(2)}) collective-permute-start(bf16[2,128,128]{2,1,0:T(8,128)(2,1)S(1)} %get-tuple-element.16), channel_id=1, source_target_pairs={{0,2},{1,3},{2,0},{3,1},{4,6},{5,7},{6,4},{7,5},{8,10},{9,11},{10,... | collective-permute-start | bytes 196616 | tf_op jit(solution)/shard_map/ppermute | solution.py:22
  22.9 1.4 collective-permute-start.4
  24.4 8.4 %collective-permute-start.5 = (bf16[8,128,128]{2,1,0:T(8,128)(2,1)S(1)}, bf16[8,128,128]{2,1,0:T(8,128)(2,1)S(1)}, u32[]{:S(2)}, u32[]{:S(2)}) collective-permute-start(bf16[8,128,128]{2,1,0:T(8,128)(2,1)S(1)} %bitcast.147), channel_id=1, source_target_pairs={{0,8},{1,9},{2,10},{3,11},{4,12},{5,13},{6,14},{7,15},{8,0},{9,1},... | collective-permute-start | bytes 786440 | tf_op jit(solution)/shard_map/ppermute | solution.py:22
  33.1 13.3 %collective-permute-start.6 = (bf16[16,128,128]{2,1,0:T(8,128)(2,1)S(1)}, bf16[16,128,128]{2,1,0:T(8,128)(2,1)}, u32[]{:S(2)}, u32[]{:S(2)}) collective-permute-start(bf16[16,128,128]{2,1,0:T(8,128)(2,1)S(1)} %bitcast.142), channel_id=1, source_target_pairs={{0,16},{1,17},{2,18},{3,19},{4,20},{5,21},{6,22},{7,23},{8,24},{9,... | collective-permute-start | bytes 1572872 | tf_op jit(solution)/shard_map/ppermute | solution.py:22
  34.8 2.6 %copy-start = (bf16[8,10,128,128]{3,2,1,0:T(8,128)(2,1)S(1)}, bf16[8,10,128,128]{3,2,1,0:T(8,128)(2,1)}, u32[]{:S(2)}) copy-start(bf16[8,10,128,128]{3,2,1,0:T(8,128)(2,1)} %param.10) | copy-start | bytes 7864324
  47.5 4.5 %copy-start.4 = (f32[8,128]{1,0:T(8,128)S(1)}, f32[8,128]{1,0:T(8,128)}, u32[]{:S(2)}) copy-start(f32[8,128]{1,0:T(8,128)} %add.94) | copy-start | bytes 12292
  52.0 2.6 %copy-start.1 = (bf16[1024,128]{1,0:T(8,128)(2,1)S(1)}, bf16[1024,128]{1,0:T(8,128)(2,1)}, u32[]{:S(2)}) copy-start(bf16[1024,128]{1,0:T(8,128)(2,1)} %param.7) | copy-start | bytes 786436
  55.5 4.0 %collective-permute-start.9 = (bf16[1,128,128]{2,1,0:T(8,128)(2,1)S(1)}, bf16[1,128,128]{2,1,0:T(8,128)(2,1)S(1)}, u32[]{:S(2)}, u32[]{:S(2)}) collective-permute-start(bf16[1,128,128]{2,1,0:T(8,128)(2,1)S(1)} %bitcast.166), channel_id=1, source_target_pairs={{0,1},{1,0},{2,3},{3,2},{4,5},{5,4},{6,7},{7,6},{8,9},{9,8},{10,11... | collective-permute-start | bytes 98312 | tf_op jit(solution)/shard_map/ppermute | solution.py:22
  59.6 5.2 %collective-permute-start.10 = (bf16[2,128,128]{2,1,0:T(8,128)(2,1)S(1)}, bf16[2,128,128]{2,1,0:T(8,128)(2,1)S(1)}, u32[]{:S(2)}, u32[]{:S(2)}) collective-permute-start(bf16[2,128,128]{2,1,0:T(8,128)(2,1)S(1)} %get-tuple-element.14), channel_id=1, source_target_pairs={{0,2},{1,3},{2,0},{3,1},{4,6},{5,7},{6,4},{7,5},{8,10},{9,11},{10,... | collective-permute-start | bytes 196616 | tf_op jit(solution)/shard_map/ppermute | solution.py:22
  64.8 1.4 collective-permute-start.11
  66.4 8.4 %collective-permute-start.12 = (bf16[8,128,128]{2,1,0:T(8,128)(2,1)S(1)}, bf16[8,128,128]{2,1,0:T(8,128)(2,1)S(1)}, u32[]{:S(2)}, u32[]{:S(2)}) collective-permute-start(bf16[8,128,128]{2,1,0:T(8,128)(2,1)S(1)} %bitcast.151), channel_id=1, source_target_pairs={{0,8},{1,9},{2,10},{3,11},{4,12},{5,13},{6,14},{7,15},{8,0},{9,1},... | collective-permute-start | bytes 786440 | tf_op jit(solution)/shard_map/ppermute | solution.py:22
  68.1 10.0 %collective-permute-start.8 = (bf16[256,128]{1,0:T(8,128)(2,1)S(1)}, bf16[256,128]{1,0:T(8,128)(2,1)S(1)}, u32[]{:S(2)}, u32[]{:S(2)}) collective-permute-start(bf16[256,128]{1,0:T(8,128)(2,1)S(1)} %get-tuple-element.8), channel_id=1, source_target_pairs={{1,0},{2,1},{3,2},{4,3},{5,4},{6,5},{7,6},{8,7},{9,8},{10,9},{11,1... | collective-permute-start | bytes 196616 | tf_op jit(solution)/shard_map/ppermute | solution.py:37
  69.4 8.7 %collective-permute-start.7 = (bf16[256,128]{1,0:T(8,128)(2,1)S(1)}, bf16[256,128]{1,0:T(8,128)(2,1)S(1)}, u32[]{:S(2)}, u32[]{:S(2)}) collective-permute-start(bf16[256,128]{1,0:T(8,128)(2,1)S(1)} %get-tuple-element.7), channel_id=1, source_target_pairs={{0,1},{1,2},{2,3},{3,4},{4,5},{5,6},{6,7},{7,8},{8,9},{9,10},{10,1... | collective-permute-start | bytes 196616 | tf_op jit(solution)/shard_map/ppermute | solution.py:34
  75.7 15.2 %collective-permute-start.13 = (bf16[16,128,128]{2,1,0:T(8,128)(2,1)}, bf16[16,128,128]{2,1,0:T(8,128)(2,1)}, u32[]{:S(2)}, u32[]{:S(2)}) collective-permute-start(bf16[16,128,128]{2,1,0:T(8,128)(2,1)} %bitcast.43), channel_id=1, source_target_pairs={{0,16},{1,17},{2,18},{3,19},{4,20},{5,21},{6,22},{7,23},{8,24},{9,... | collective-permute-start | bytes 1572872 | tf_op jit(solution)/shard_map/ppermute | solution.py:22
  92.3 4.5 %copy-start.5 = (f32[8,128]{1,0:T(8,128)S(1)}, f32[8,128]{1,0:T(8,128)}, u32[]{:S(2)}) copy-start(f32[8,128]{1,0:T(8,128)} %add.94) | copy-start | bytes 12292
  100.3 4.0 %collective-permute-start.16 = (bf16[1,128,128]{2,1,0:T(8,128)(2,1)S(1)}, bf16[1,128,128]{2,1,0:T(8,128)(2,1)S(1)}, u32[]{:S(2)}, u32[]{:S(2)}) collective-permute-start(bf16[1,128,128]{2,1,0:T(8,128)(2,1)S(1)} %bitcast.164), channel_id=1, source_target_pairs={{0,1},{1,0},{2,3},{3,2},{4,5},{5,4},{6,7},{7,6},{8,9},{9,8},{10,11... | collective-permute-start | bytes 98312 | tf_op jit(solution)/shard_map/ppermute | solution.py:22
  104.3 5.3 %collective-permute-start.17 = (bf16[2,128,128]{2,1,0:T(8,128)(2,1)S(1)}, bf16[2,128,128]{2,1,0:T(8,128)(2,1)S(1)}, u32[]{:S(2)}, u32[]{:S(2)}) collective-permute-start(bf16[2,128,128]{2,1,0:T(8,128)(2,1)S(1)} %get-tuple-element.12), channel_id=1, source_target_pairs={{0,2},{1,3},{2,0},{3,1},{4,6},{5,7},{6,4},{7,5},{8,10},{9,11},{10,... | collective-permute-start | bytes 196616 | tf_op jit(solution)/shard_map/ppermute | solution.py:22
  109.6 1.4 collective-permute-start.18
  111.1 8.4 %collective-permute-start.19 = (bf16[8,128,128]{2,1,0:T(8,128)(2,1)S(1)}, bf16[8,128,128]{2,1,0:T(8,128)(2,1)S(1)}, u32[]{:S(2)}, u32[]{:S(2)}) collective-permute-start(bf16[8,128,128]{2,1,0:T(8,128)(2,1)S(1)} %bitcast.149), channel_id=1, source_target_pairs={{0,8},{1,9},{2,10},{3,11},{4,12},{5,13},{6,14},{7,15},{8,0},{9,1},... | collective-permute-start | bytes 786440 | tf_op jit(solution)/shard_map/ppermute | solution.py:22
  112.3 10.6 %collective-permute-start.15 = (bf16[256,128]{1,0:T(8,128)(2,1)S(1)}, bf16[256,128]{1,0:T(8,128)(2,1)S(1)}, u32[]{:S(2)}, u32[]{:S(2)}) collective-permute-start(bf16[256,128]{1,0:T(8,128)(2,1)S(1)} %get-tuple-element.6), channel_id=1, source_target_pairs={{1,0},{2,1},{3,2},{4,3},{5,4},{6,5},{7,6},{8,7},{9,8},{10,9},{11,1... | collective-permute-start | bytes 196616 | tf_op jit(solution)/shard_map/ppermute | solution.py:37
  113.6 9.3 %collective-permute-start.14 = (bf16[256,128]{1,0:T(8,128)(2,1)S(1)}, bf16[256,128]{1,0:T(8,128)(2,1)S(1)}, u32[]{:S(2)}, u32[]{:S(2)}) collective-permute-start(bf16[256,128]{1,0:T(8,128)(2,1)S(1)} %get-tuple-element.5), channel_id=1, source_target_pairs={{0,1},{1,2},{2,3},{3,4},{4,5},{5,6},{6,7},{7,8},{8,9},{9,10},{10,1... | collective-permute-start | bytes 196616 | tf_op jit(solution)/shard_map/ppermute | solution.py:34
  120.5 15.1 %collective-permute-start.20 = (bf16[16,128,128]{2,1,0:T(8,128)(2,1)}, bf16[16,128,128]{2,1,0:T(8,128)(2,1)}, u32[]{:S(2)}, u32[]{:S(2)}) collective-permute-start(bf16[16,128,128]{2,1,0:T(8,128)(2,1)} %bitcast.68), channel_id=1, source_target_pairs={{0,16},{1,17},{2,18},{3,19},{4,20},{5,21},{6,22},{7,23},{8,24},{9,... | collective-permute-start | bytes 1572872 | tf_op jit(solution)/shard_map/ppermute | solution.py:22
  136.9 2.3 %copy-start.6 = (f32[8,128]{1,0:T(8,128)S(1)}, f32[8,128]{1,0:T(8,128)}, u32[]{:S(2)}) copy-start(f32[8,128]{1,0:T(8,128)} %add.94) | copy-start | bytes 12292
  137.2 2.0 %copy-start.3 = (bf16[8,6,128,128]{3,2,1,0:T(8,128)(2,1)S(1)}, bf16[8,6,128,128]{3,2,1,0:T(8,128)(2,1)}, u32[]{:S(2)}) copy-start(bf16[8,6,128,128]{3,2,1,0:T(8,128)(2,1)} %param.12) | copy-start | bytes 4718596
